TPU v7x, 128 devices: a whole 4x4x4 slice. The times are simulated.
128 devices in a mesh: fsdp: 16 (over z, x_lo, core), seq: 8 (over x_hi, y).
Axes of the slice: x: 4 (x_hi: 2, x_lo: 2; x = x_hi * 2 + x_lo), y: 4, z: 4, core: 2. Of those that a mesh axis runs over, the one named last changes fastest.
Arguments:
- hidden_in: bfloat16 [64, 5, 1536], P('fsdp'), may hold values from -6 to 6
- norm_gain: float32 [1536], replicated, may hold values from 0.1 to 1.9
- w_qkv: bfloat16 [1536, 3, 24, 64], P(None, None, 'seq', 'fsdp'), may hold values from -0.15625 to 0.15625
- w_forget: bfloat16 [1536, 24], replicated, may hold values from -0.15625 to 0.15625
- forget_bias: float32 [24], replicated, may hold values from 1 to 5
- cache_keys: bfloat16 [64, 4096, 1536], P('fsdp', 'seq')
- cache_values: bfloat16 [64, 4096, 1536], P('fsdp', 'seq'), may hold values from -6 to 6
- cache_forget: float32 [64, 24, 4096], P('fsdp', None, 'seq')
- cache_lengths: int32 [64], P('fsdp'), may hold values from 128 to 4096, as said below
- piece_map: int32 [64, 8], P('fsdp'), may hold values from 0 to 7, each once within a row
- draft_counts: int32 [64], P('fsdp'), may hold values from 1 to 4
Outputs:
- verified: bfloat16 [64, 5, 1536], P('fsdp', None, 'seq')
Inputs may be any that keep to these rules, and one draw needn't show every extreme that they name: `cache_lengths`: 16 requests drawn at random have lengths from 3841 to 4096, one exactly 4096; the others have lengths from 128 to 256, one exactly 128.
All inputs are finite; a program needn't handle non-finite values.
Results may differ from a plain program's by a relative error of at most 0.012.
The roundings to bfloat16 on the way count: a program that leaves them out, or rounds other values in their place, can miss the bound.
Values may be sent and summed in bfloat16 or wider, within the bound.
No kernel may reach another device: no remote copies, remote signals or barrier semaphores. Data moves between devices by JAX's collectives and lax.ppermute only.
A program may use at most 128 MiB of HBM per device.

v0:
```python
import jax
import jax.numpy as jnp
from jax import lax
from jax.sharding import PartitionSpec as P

HEAD_DIM = 64
norm_eps = 1e-06
neg_fill = -1e30


def normalize(rows, gain):
    values = rows.astype(jnp.float32)
    mean_sq = jnp.mean(values * values, axis=-1, keepdims=True)
    return (values * lax.rsqrt(mean_sq + norm_eps) * gain).astype(jnp.bfloat16)


def fold_parts(parts):
    maxima, sums, accums = parts
    joint = jnp.max(maxima, axis=0)
    factor = jnp.exp(maxima - joint[None])
    return (joint, jnp.sum(sums * factor, axis=0), jnp.sum(accums * factor[..., None], axis=0))


def body(
    hidden_in,
    norm_gain,
    w_qkv,
    w_forget,
    forget_bias,
    cache_keys,
    cache_values,
    cache_forget,
    cache_lengths,
    piece_map,
    draft_counts,
):
    req_count, new_count, width = hidden_in.shape
    head_count = w_forget.shape[1]
    seq_count = lax.axis_size("seq")
    own_heads = w_qkv.shape[2]
    own_width = own_heads * HEAD_DIM
    piece_len = cache_forget.shape[2]
    logit_scale = HEAD_DIM ** (-0.5)
    seq_index = lax.axis_index("seq")
    head_start = seq_index * own_heads
    normed = normalize(hidden_in, norm_gain).reshape(req_count * new_count, width)
    gate_logit = (
        jnp.dot(normed, w_forget, preferred_element_type=jnp.float32).reshape(
            req_count, new_count, head_count
        )
        + forget_bias
    )
    prefix = jnp.cumsum(jax.nn.log_sigmoid(gate_logit), axis=1)
    projected = jnp.einsum(
        "nd,dchk->nchk",
        normed,
        lax.all_gather(w_qkv, "fsdp", axis=3, tiled=True),
        preferred_element_type=jnp.float32,
    ).astype(jnp.bfloat16)
    own_part = projected.reshape(req_count * new_count, 3, own_width)
    all_heads = lax.all_gather(own_part, "seq", axis=2, tiled=True).reshape(
        req_count, new_count, 3, head_count, HEAD_DIM
    )
    query_rows_all = all_heads[:, :, 0]
    slot_ids = jnp.arange(seq_count, dtype=jnp.int32)
    holders = piece_map[:, :, None] == slot_ids[None, None, :]
    piece_of_slot = jnp.sum(jnp.where(holders, slot_ids[None, :, None], 0), axis=1)
    own_piece = jnp.sum(jnp.where(piece_map == seq_index, slot_ids[None, :], 0), axis=1)
    positions = own_piece[:, None] * piece_len + jnp.arange(piece_len, dtype=jnp.int32)[None, :]
    live_mask = positions < cache_lengths[:, None]
    masked = jnp.where(live_mask[:, None, :], cache_forget, 0.0)
    piece_total = jnp.sum(masked, axis=-1)
    all_totals = lax.all_gather(piece_total[None], "seq", axis=0, tiled=True)
    later_piece = (piece_of_slot.T > own_piece[None, :])[:, :, None]
    later_sum = jnp.sum(jnp.where(later_piece, all_totals, 0.0), axis=0)
    trailing_part = piece_total[..., None] - jnp.cumsum(masked, axis=-1) + later_sum[..., None]
    key_rows = cache_keys.reshape(req_count, piece_len, head_count, HEAD_DIM)
    value_rows = cache_values.reshape(req_count, piece_len, head_count, HEAD_DIM)
    prefix_transposed = jnp.transpose(prefix, (0, 2, 1))
    scores = (
        jnp.einsum("rmhd,rthd->rhmt", query_rows_all, key_rows, preferred_element_type=jnp.float32)
        * logit_scale
    )
    scores = scores + trailing_part[:, :, None, :] + prefix_transposed[..., None]
    key_live = live_mask[:, None, None, :]
    row_max = jnp.max(jnp.where(key_live, scores, neg_fill), axis=-1)
    attn_weights = jnp.where(key_live, jnp.exp(scores - row_max[..., None]), 0.0)
    weight_sum = jnp.sum(attn_weights, axis=-1)
    accum = jnp.einsum(
        "rhmt,rthd->rhmd",
        attn_weights.astype(jnp.bfloat16),
        value_rows,
        preferred_element_type=jnp.float32,
    )
    gathered = (
        lax.all_gather(row_max[None], "seq", axis=0, tiled=True),
        lax.all_gather(weight_sum[None], "seq", axis=0, tiled=True),
        lax.all_gather(accum[None], "seq", axis=0, tiled=True),
    )
    own_parts = tuple(
        (lax.dynamic_slice_in_dim(member, head_start, own_heads, 2) for member in gathered)
    )
    cache_max, cache_sum, cache_acc = fold_parts(own_parts)
    own_rows = own_part.reshape(req_count, new_count, 3, own_heads, HEAD_DIM)
    own_prefix = jnp.transpose(
        lax.dynamic_slice_in_dim(prefix, head_start, own_heads, 2), (0, 2, 1)
    )
    fresh_logits = (
        jnp.einsum(
            "rmhd,rnhd->rhmn",
            own_rows[:, :, 0],
            own_rows[:, :, 1],
            preferred_element_type=jnp.float32,
        )
        * logit_scale
    )
    fresh_logits = fresh_logits + own_prefix[..., :, None] - own_prefix[..., None, :]
    step_ids = jnp.arange(new_count, dtype=jnp.int32)
    causal = (step_ids[None, :] <= step_ids[:, None])[None, None]
    joint_max = jnp.maximum(cache_max, jnp.max(jnp.where(causal, fresh_logits, neg_fill), axis=-1))
    new_weights = jnp.where(causal, jnp.exp(fresh_logits - joint_max[..., None]), 0.0)
    carried = jnp.exp(cache_max - joint_max)
    total_sum = cache_sum * carried + jnp.sum(new_weights, axis=-1)
    blend_weights = cache_acc * carried[..., None] + jnp.einsum(
        "rhmn,rnhd->rhmd",
        new_weights.astype(jnp.bfloat16),
        own_rows[:, :, 2],
        preferred_element_type=jnp.float32,
    )
    result = blend_weights / total_sum[..., None]
    live_rows = (step_ids[None, :] <= draft_counts[:, None])[:, None, :, None]
    result = jnp.where(live_rows, result, 0.0)
    return (
        jnp.transpose(result, (0, 2, 1, 3))
        .reshape(req_count, new_count, own_heads * HEAD_DIM)
        .astype(jnp.bfloat16)
    )


def solution(mesh):
    in_specs = (
        P("fsdp", None, None),
        P(),
        P(None, None, "seq", "fsdp"),
        P(),
        P(),
        P("fsdp", "seq", None),
        P("fsdp", "seq", None),
        P("fsdp", None, "seq"),
        P("fsdp"),
        P("fsdp", None),
        P("fsdp"),
    )
    out_specs = P("fsdp", None, "seq")
    return jax.shard_map(body, mesh=mesh, in_specs=in_specs, out_specs=out_specs, check_vma=False)
```

profile of v0, /device:TPU:0, one launch (start us, length us, event | category | flops | bytes accessed | tf_op | source)
XLA Modules:
  0.0 235.4 jit_solution(12560561197507895507)
XLA Ops:
  6.5 0.0 copy-start
  6.5 0.0 all-gather.7.cloned.1.call-start
  6.5 1.6 copy.152
  8.2 0.0 all-gather.7.cloned.1.call-update
  8.2 0.9 fusion.14
  9.2 0.9 fusion.16
  10.1 0.0 copy-done
  10.1 0.8 fusion.34
  11.0 0.1 dynamic-slice_bitcast_fusion
  11.1 0.1 copy.171
  11.2 0.1 copy.172
  11.4 0.8 select_reduce_fusion.5
  12.2 0.8 select_reduce_fusion.4
  12.9 0.1 compare_bitcast_fusion
  13.0 0.1 copy.161
  13.1 0.7 add_compare_fusion
  13.8 1.0 select_reduce_fusion.1
  14.9 4.6 %reduce-window.6 = f32[4,24,4,128]{3,1,2,0:T(8,128)S(1)} reduce-window(f32[4,24,4,128]{3,1,2,0:T(8,128)S(1)} %bitcast.84, f32[]{:T(128)} %constant.8.clone.1), window={size=1x1x1x128 pad=0_0x0_0x0_0x127_0}, to_apply=%region_3.4 | reduce-window | flops 6242304 | bytes 393220 | tf_op jit(solution)/shard_map/reduce-window
  19.5 0.2 slice_reduce_fusion
  19.8 0.1 copy.162
  19.9 8.8 %copy.158 = bf16[4,512,1536]{1,2,0:T(8,128)(2,1)} copy(bf16[4,512,1536]{2,1,0:T(8,128)(2,1)} %param.16) | data formatting | bytes 12582912 | tf_op args[5]
  28.7 0.0 copy-start.1
  28.7 8.7 %copy.163 = bf16[4,512,1536]{1,2,0:T(8,128)(2,1)} copy(bf16[4,512,1536]{2,1,0:T(8,128)(2,1)} %param.17) | data formatting | bytes 12582912 | tf_op args[6]
  37.4 30.2 %all-gather.4 = f32[8,4,24]{2,1,0:T(4,128)S(1)} all-gather(f32[1,4,24]{2,1,0:T(4,128)S(1)} %bitcast.88), channel_id=2, replica_groups=mesh['fsdp'=16,'seq'=8] {'seq'}, dimensions={0}, use_global_device_ids=true | all-gather | bytes 3456 | tf_op jit(solution)/shard_map/all_gather | solution.py:73
  67.6 0.1 select_reduce_fusion.3
  67.7 0.0 copy-done.1
  67.8 0.1 fusion.13
  67.9 0.0 all-gather.7.cloned.1.call-done
  67.9 2.4 %fusion.4 = bf16[20,3,3,64]{3,0,2,1:T(8,128)(2,1)S(1)} fusion(bf16[1536,3,3,64]{0,2,1,3:T(4,128)(2,1)} %all-gather.7.cloned.1.call-done, bf16[20,1536,1,1]{1,0,2,3:T(8,128)(2,1)S(1)} %reshape.189), kind=kOutput, calls=%fused_computation.7 | convolution fusion | flops 35400960 | bytes 1853952 | tf_op jit(solution)/shard_map/nd,dchk->nchk/dot_general | solution.py:54
  70.4 0.2 copy.188
  70.6 0.1 fusion.21
  70.8 0.2 copy.170
  70.9 0.2 select_reduce_fusion.2
  71.1 0.1 copy.177
  71.2 0.1 copy.174
  71.3 38.0 %all_gather.19 = bf16[20,3,1536]{0,1,2:T(4,128)(2,1)S(1)} all-gather(bf16[20,3,192]{0,1,2:T(4,128)(2,1)S(1)} %bitcast.83), channel_id=1, replica_groups=mesh['fsdp'=16,'seq'=8] {'seq'}, dimensions={2}, use_global_device_ids=true | all-gather | bytes 207360 | tf_op jit(solution)/shard_map/all_gather | solution.py:61
  109.3 0.9 copy.156
  110.2 0.2 reshape.177
  110.5 3.9 %select_reduce_fusion = (f32[4,24,5]{2,1,0:T(8,128)S(1)}, f32[4,24,5,512]{3,2,1,0:T(8,128)S(1)}) fusion(pred[4,512]{1,0:T(4,128)(4,1)S(1)} %add_compare_fusion, f32[4,24,5]{2,1,0:T(8,128)S(1)} %copy.162, f32[4,24,512]{2,1,0:T(8,128)S(1)} %fusion.13, bf16[4,512,24,64]{1,3,2,0:T(8,128)(2,1)} %bitcast.78, bf16[4,5,1,24,64]{4,3,1,0,2:T(8,128)(2,1)S(1)} %slice.24), kind=kOutput, calls=%fused_computation.3 | convolution fusion | flops 32685600 | bytes 7538432 | tf_op jit(solution)/shard_map/rmhd,rthd->rhmt/dot_general | solution.py:81
  114.3 0.1 copy.165
  114.4 0.5 fusion.2
  114.9 0.1 copy.182
  115.0 34.2 %all-gather.3 = f32[32,24,5]{1,2,0:T(8,128)S(1)} all-gather(f32[4,24,5]{1,2,0:T(8,128)S(1)} %copy.182), channel_id=5, replica_groups=mesh['fsdp'=16,'seq'=8] {'seq'}, dimensions={0}, use_global_device_ids=true | all-gather | bytes 17280 | tf_op jit(solution)/shard_map/all_gather | solution.py:97
  149.2 34.2 %all-gather.2 = f32[32,24,5]{1,2,0:T(8,128)S(1)} all-gather(f32[4,24,5]{1,2,0:T(8,128)S(1)} %copy.165), channel_id=4, replica_groups=mesh['fsdp'=16,'seq'=8] {'seq'}, dimensions={0}, use_global_device_ids=true | all-gather | bytes 17280 | tf_op jit(solution)/shard_map/all_gather | solution.py:96
  183.4 0.1 dynamic-slice_reduce_fusion
  183.6 0.1 copy.176
  183.7 0.1 multiply_reduce_fusion.1
  183.8 0.1 copy.178
  183.9 0.2 fusion.37
  184.1 0.1 copy.184
  184.3 0.1 copy.175
  184.4 0.1 copy.185
  184.5 4.6 %fusion.8 = f32[4,24,5,64]{3,2,1,0:T(8,128)S(1)} fusion(bf16[4,512,24,64]{1,3,2,0:T(8,128)(2,1)} %bitcast.79, f32[4,24,5,512]{3,2,1,0:T(8,128)S(1)} %get-tuple-element.19, f32[4,24,5]{2,1,0:T(8,128)S(1)} %get-tuple-element.18, pred[4,512]{1,0:T(4,128)(4,1)S(1)} %add_compare_fusion), kind=kOutput, calls=%fused_computation.10 | convolution fusion | flops 32194560 | bytes 7401344 | tf_op jit(solution)/shard_map/rhmt,rthd->rhmd/dot_general | solution.py:89
  189.1 0.1 copy.164
  189.1 38.2 %all-gather.1 = f32[32,24,5,64]{3,1,2,0:T(8,128)S(1)} all-gather(f32[4,24,5,64]{3,1,2,0:T(8,128)S(1)} %copy.164), channel_id=3, replica_groups=mesh['fsdp'=16,'seq'=8] {'seq'}, dimensions={0}, use_global_device_ids=true | all-gather | bytes 1105920 | tf_op jit(solution)/shard_map/all_gather | solution.py:98
  227.4 0.3 multiply_reduce_fusion
  227.6 0.1 fusion.20
  227.8 0.1 select_convert_fusion
  227.9 0.7 convert_element_type.27
  (17 shorter events, 0.3 us)
Async XLA Ops:
  6.5 3.6 %copy-start = (bf16[1536,24]{0,1:T(8,128)(2,1)S(1)}, bf16[1536,24]{0,1:T(8,128)(2,1)}, u32[]{:S(2)}) copy-start(bf16[1536,24]{0,1:T(8,128)(2,1)} %param.14) | copy-start | bytes 221188
  6.5 61.4 %all-gather.7.cloned.1.call-start = ((), (), s32[]{:S(2)}) async-start(), calls=%async_computation | async-start | bytes 2506752 | tf_op jit(solution)/shard_map/all_gather | solution.py:57
  28.7 39.0 %copy-start.1 = (s32[4]{0:T(128)S(1)}, s32[4]{0:T(128)}, u32[]{:S(2)}) copy-start(s32[4]{0:T(128)} %param.21) | copy-start | bytes 52
Sparse Core Ops, SparseCore 0:
  9.1 37.0 all-gather.6
where the time goes:
time: 236 us; the launch traced here: 235 us
  blocking collectives  175 us (74%)
  local copies, waits for them, and re-layouts  23.3 us (10%)
  between operations  13.6 us (6%)
  matrix products  12 us (5%)
  other arithmetic  11.7 us (5%)
    all_gather x1, blocking collectives, body(): lax.all_gather(accum[None], 'seq', axis=0, tiled=True)  38.2 us
    all_gather x1, blocking collectives, body(): lax.all_gather(own_part, 'seq', axis=2, tiled=True)  38 us
    all_gather x1, blocking collectives, body(): lax.all_gather(row_max[None], 'seq', axis=0, tiled=True)  34.2 us
    all_gather x1, blocking collectives, body(): lax.all_gather(weight_sum[None], 'seq', axis=0, tiled=True)  34.2 us
    all_gather x1, blocking collectives, body(): all_totals = lax.all_gather(piece_total[None], 'seq', axis=0, tiled=True)  30.2 us
    unnamed x7, local copies, waits for them, and re-layouts  19.1 us
  transfers between devices with their start and end apart: 1, of which 0 were waited for; matrix products, arithmetic and copies ran while one was open for 12% of the time, Pallas kernels for 0%

commit v1 on v0

--- a/solution.py
+++ b/solution.py
@@ -70,7 +70,11 @@
     live_mask = positions < cache_lengths[:, None]
     masked = jnp.where(live_mask[:, None, :], cache_forget, 0.0)
     piece_total = jnp.sum(masked, axis=-1)
-    all_totals = lax.all_gather(piece_total[None], "seq", axis=0, tiled=True)
+    part = piece_total[None]
+    size = lax.axis_size("seq")
+    tiles = jnp.stack([part for _ in range(size)])
+    tiles = lax.all_to_all(tiles, "seq", split_axis=0, concat_axis=0)
+    all_totals = jnp.concatenate(tiles, axis=0)
     later_piece = (piece_of_slot.T > own_piece[None, :])[:, :, None]
     later_sum = jnp.sum(jnp.where(later_piece, all_totals, 0.0), axis=0)
     trailing_part = piece_total[..., None] - jnp.cumsum(masked, axis=-1) + later_sum[..., None]

time: 236 us -> 214 us (0.907)
  blocking collectives: 175 us -> 144 us
  starting transfers between devices: 0.01 us -> 7.05 us
  waiting for transfers between devices: 0.04 us -> 3.93 us
    all_gather x1 -> x0, blocking collectives: 30.2 us -> none  [body(): all_totals = lax.all_gather(piece_total[None], 'seq', axis=0, tiled=True)]
    all_to_all x0 -> x1, starting transfers between devices: none -> 7.01 us  [body(): tiles = lax.all_to_all(tiles, 'seq', split_axis=0, concat_axis=0)]
    all_gather x1, waiting for transfers between devices: 0.02 us -> 3.91 us  [body(): lax.all_gather(w_qkv, 'fsdp', axis=3, tiled=True)]
    unnamed x7 -> x15, local copies, waits for them, and re-layouts: 19.1 us -> 19.1 us
  transfers between devices with their start and end apart: 1 -> 2, of which waited for: 0 -> 1; matrix products, arithmetic and copies ran while one was open for 12% -> 13% of each run, Pallas kernels for 0% -> 0%
where the time goes in v1:
time: 214 us; the launch traced here: 213 us
  blocking collectives  144 us (67%)
  local copies, waits for them, and re-layouts  23.8 us (11%)
  between operations  13.6 us (6%)
  matrix products  11.3 us (5%)
  other arithmetic  9.36 us (4%)
  starting transfers between devices  7.05 us (3%)
  waiting for transfers between devices  3.93 us (2%)
    all_gather x1, blocking collectives, body(): lax.all_gather(accum[None], 'seq', axis=0, tiled=True)  38.2 us
    all_gather x1, blocking collectives, body(): lax.all_gather(own_part, 'seq', axis=2, tiled=True)  37.7 us
    all_gather x1, blocking collectives, body(): lax.all_gather(weight_sum[None], 'seq', axis=0, tiled=True)  34.2 us
    all_gather x1, blocking collectives, body(): lax.all_gather(row_max[None], 'seq', axis=0, tiled=True)  34.2 us
    unnamed x15, local copies, waits for them, and re-layouts  19.1 us
    all_to_all x1, starting transfers between devices, body(): tiles = lax.all_to_all(tiles, 'seq', split_axis=0, concat_axis=0)  7.01 us
    another operation x2, other arithmetic  4.64 us
    dot_general x1, matrix products, body(): jnp.einsum('rhmt,rthd->rhmd', attn_weights.astype(jnp.bfloat16), value_ro...  4.57 us
  transfers between devices with their start and end apart: 2, of which 1 were waited for; matrix products, arithmetic and copies ran while one was open for 13% of the time, Pallas kernels for 0%

profile of v1, /device:TPU:0, one launch (start us, length us, event | category | flops | bytes accessed | tf_op | source)
XLA Modules:
  0.0 213.4 jit_solution(2983240989300911069)
XLA Ops:
  6.5 0.0 copy-start
  6.5 0.0 copy-start.5
  6.6 0.0 all-gather.5.cloned.1.call-start
  6.6 1.7 copy.154
  8.3 0.0 all-gather.5.cloned.1.call-update
  8.3 0.8 select_reduce_fusion.4
  9.1 0.7 add_compare_fusion
  9.8 1.0 select_reduce_fusion.1
  10.9 0.6 stack.3
  11.5 7.0 %all-to-all-start = ((f32[8,1,4,24]{3,2,1,0:T(4,128)}), f32[8,1,4,24]{3,2,1,0:T(4,128)S(1)}, u32[]{:S(2)}, u32[]{:S(2)}) async-start(f32[8,1,4,24]{3,2,1,0:T(4,128)} %stack.3), calls=%async_computation | async-start | bytes 32768 | tf_op jit(solution)/shard_map/all_to_all | solution.py:76
  18.5 4.6 %reduce-window.6 = f32[4,24,4,128]{3,1,2,0:T(8,128)S(1)} reduce-window(f32[4,24,4,128]{3,1,2,0:T(8,128)S(1)} %bitcast.87, f32[]{:T(128)} %constant.8.clone.1), window={size=1x1x1x128 pad=0_0x0_0x0_0x127_0}, to_apply=%region_3.4 | reduce-window | flops 6242304 | bytes 393220 | tf_op jit(solution)/shard_map/reduce-window
  23.1 0.0 copy-done.1
  23.1 0.1 fusion.14
  23.2 0.0 copy-done.2
  23.2 0.1 fusion.16
  23.3 0.0 copy-done
  23.4 0.0 copy-done.4
  23.4 0.2 fusion.35
  23.6 0.1 dynamic-slice_bitcast_fusion
  23.7 0.0 copy-done.3
  23.7 0.1 select_reduce_fusion.3
  23.8 0.2 slice_reduce_fusion
  24.0 0.1 compare_bitcast_fusion
  24.1 0.1 copy.173
  24.3 0.1 copy.174
  24.4 0.1 copy.163
  24.5 0.1 copy.164
  24.6 8.7 %copy.160 = bf16[4,512,1536]{1,2,0:T(8,128)(2,1)} copy(bf16[4,512,1536]{2,1,0:T(8,128)(2,1)} %param.16) | data formatting | bytes 12582912 | tf_op args[5]
  33.4 8.7 %copy.165 = bf16[4,512,1536]{1,2,0:T(8,128)(2,1)} copy(bf16[4,512,1536]{2,1,0:T(8,128)(2,1)} %param.17) | data formatting | bytes 12582912 | tf_op args[6]
  42.0 0.0 all-to-all-done
  42.1 0.1 fusion.24
  42.1 0.1 fusion.13
  42.3 3.9 %all-gather.5.cloned.1.call-done = bf16[1536,3,3,64]{0,2,1,3:T(4,128)(2,1)} async-done(((bf16[1536,3,3,4]{0,2,1,3:T(4,128)(2,1)}), bf16[1536,3,3,64]{0,2,1,3:T(4,128)(2,1)}) %all-gather.5.cloned.1.call-update) | async-done | bytes 1769488 | tf_op jit(solution)/shard_map/all_gather | solution.py:57
  46.2 2.4 %fusion.4 = bf16[20,3,3,64]{3,0,2,1:T(8,128)(2,1)S(1)} fusion(bf16[1536,3,3,64]{0,2,1,3:T(4,128)(2,1)} %all-gather.5.cloned.1.call-done, bf16[20,1536,1,1]{1,0,2,3:T(8,128)(2,1)S(1)} %reshape.191), kind=kOutput, calls=%fused_computation.7 | convolution fusion | flops 35400960 | bytes 1853952 | tf_op jit(solution)/shard_map/nd,dchk->nchk/dot_general | solution.py:54
  48.6 0.2 copy.190
  48.9 0.1 fusion.21
  49.0 0.2 copy.172
  49.2 0.2 select_reduce_fusion.2
  49.4 0.1 copy.179
  49.5 0.1 copy.176
  49.6 37.7 %all_gather.16 = bf16[20,3,1536]{0,1,2:T(4,128)(2,1)S(1)} all-gather(bf16[20,3,192]{0,1,2:T(4,128)(2,1)S(1)} %bitcast.86), channel_id=1, replica_groups=mesh['fsdp'=16,'seq'=8] {'seq'}, dimensions={2}, use_global_device_ids=true | all-gather | bytes 207360 | tf_op jit(solution)/shard_map/all_gather | solution.py:61
  87.3 0.9 copy.158
  88.2 0.2 reshape.182
  88.5 3.9 %select_reduce_fusion = (f32[4,24,5]{2,1,0:T(8,128)S(1)}, f32[4,24,5,512]{3,2,1,0:T(8,128)S(1)}) fusion(pred[4,512]{1,0:T(4,128)(4,1)S(1)} %add_compare_fusion, f32[4,24,5]{2,1,0:T(8,128)S(1)} %copy.164, f32[4,24,512]{2,1,0:T(8,128)S(1)} %fusion.13, bf16[4,512,24,64]{1,3,2,0:T(8,128)(2,1)} %bitcast.81, bf16[4,5,1,24,64]{4,3,1,0,2:T(8,128)(2,1)S(1)} %slice.24), kind=kOutput, calls=%fused_computation.3 | convolution fusion | flops 32685600 | bytes 7538432 | tf_op jit(solution)/shard_map/rmhd,rthd->rhmt/dot_general | solution.py:85
  92.3 0.1 copy.167
  92.4 0.5 fusion.2
  92.9 0.1 copy.184
  93.0 34.2 %all-gather.2 = f32[32,24,5]{1,2,0:T(8,128)S(1)} all-gather(f32[4,24,5]{1,2,0:T(8,128)S(1)} %copy.184), channel_id=4, replica_groups=mesh['fsdp'=16,'seq'=8] {'seq'}, dimensions={0}, use_global_device_ids=true | all-gather | bytes 17280 | tf_op jit(solution)/shard_map/all_gather | solution.py:101
  127.2 34.2 %all-gather.1 = f32[32,24,5]{1,2,0:T(8,128)S(1)} all-gather(f32[4,24,5]{1,2,0:T(8,128)S(1)} %copy.167), channel_id=3, replica_groups=mesh['fsdp'=16,'seq'=8] {'seq'}, dimensions={0}, use_global_device_ids=true | all-gather | bytes 17280 | tf_op jit(solution)/shard_map/all_gather | solution.py:100
  161.4 0.1 dynamic-slice_reduce_fusion
  161.5 0.1 copy.178
  161.6 0.1 multiply_reduce_fusion.1
  161.8 0.1 copy.180
  161.9 0.2 fusion.38
  162.1 0.1 copy.186
  162.2 0.1 copy.177
  162.3 0.1 copy.187
  162.5 4.6 %fusion.8 = f32[4,24,5,64]{3,2,1,0:T(8,128)S(1)} fusion(bf16[4,512,24,64]{1,3,2,0:T(8,128)(2,1)} %bitcast.82, f32[4,24,5,512]{3,2,1,0:T(8,128)S(1)} %get-tuple-element.19, f32[4,24,5]{2,1,0:T(8,128)S(1)} %get-tuple-element.18, pred[4,512]{1,0:T(4,128)(4,1)S(1)} %add_compare_fusion), kind=kOutput, calls=%fused_computation.10 | convolution fusion | flops 32194560 | bytes 7401344 | tf_op jit(solution)/shard_map/rhmt,rthd->rhmd/dot_general | solution.py:93
  167.0 0.1 copy.166
  167.1 38.2 %all-gather = f32[32,24,5,64]{3,1,2,0:T(8,128)S(1)} all-gather(f32[4,24,5,64]{3,1,2,0:T(8,128)S(1)} %copy.166), channel_id=2, replica_groups=mesh['fsdp'=16,'seq'=8] {'seq'}, dimensions={0}, use_global_device_ids=true | all-gather | bytes 1105920 | tf_op jit(solution)/shard_map/all_gather | solution.py:102
  205.3 0.3 multiply_reduce_fusion
  205.6 0.1 fusion.20
  205.7 0.1 select_convert_fusion
  205.8 0.7 convert_element_type.27
  (22 shorter events, 0.3 us)
Async XLA Ops:
  6.5 16.8 %copy-start = (bf16[1536,24]{0,1:T(8,128)(2,1)S(1)}, bf16[1536,24]{0,1:T(8,128)(2,1)}, u32[]{:S(2)}) copy-start(bf16[1536,24]{0,1:T(8,128)(2,1)} %param.14) | copy-start | bytes 221188
  6.5 17.1 %copy-start.3 = (s32[4,8]{1,0:T(4,128)S(1)}, s32[4,8]{1,0:T(4,128)}, u32[]{:S(2)}) copy-start(s32[4,8]{1,0:T(4,128)} %param.20) | copy-start | bytes 388
  6.5 16.6 %copy-start.1 = (bf16[4,5,1536]{2,0,1:T(4,128)(2,1)S(1)}, bf16[4,5,1536]{2,0,1:T(4,128)(2,1)}, u32[]{:S(2)}) copy-start(bf16[4,5,1536]{2,0,1:T(4,128)(2,1)} %param.11) | copy-start | bytes 184324
  6.5 16.7 %copy-start.2 = (f32[1536]{0:T(1024)S(1)}, f32[1536]{0:T(1024)}, u32[]{:S(2)}) copy-start(f32[1536]{0:T(1024)} %param.12) | copy-start | bytes 18436
  6.5 16.8 %copy-start.4 = (f32[24]{0:T(128)S(1)}, f32[24]{0:T(128)}, u32[]{:S(2)}) copy-start(f32[24]{0:T(128)} %param.15) | copy-start | bytes 292
  6.5 17.4 %copy-start.5 = (s32[4]{0:T(128)S(1)}, s32[4]{0:T(128)}, u32[]{:S(2)}) copy-start(s32[4]{0:T(128)} %param.21) | copy-start | bytes 52
  6.6 39.6 %all-gather.5.cloned.1.call-start = ((), (), s32[]{:S(2)}) async-start(), calls=%async_computation.1 | async-start | bytes 2506752 | tf_op jit(solution)/shard_map/all_gather | solution.py:57
  11.5 30.6 %all-to-all-start = ((f32[8,1,4,24]{3,2,1,0:T(4,128)}), f32[8,1,4,24]{3,2,1,0:T(4,128)S(1)}, u32[]{:S(2)}, u32[]{:S(2)}) async-start(f32[8,1,4,24]{3,2,1,0:T(4,128)} %stack.3), calls=%async_computation | async-start | bytes 32768 | tf_op jit(solution)/shard_map/all_to_all | solution.py:76
Sparse Core Ops, SparseCore 0:
  9.1 37.0 all-gather.4
